TPU v7x, 256 devices: a whole 4x4x8 slice. The times are simulated.
256 devices in a mesh: req: 64 (over z, x, core), tp: 4 (over y).
Axes of the slice: x: 4, y: 4, z: 8, core: 2. Of those that a mesh axis runs over, the one named last changes fastest.
Arguments:
- hidden: bfloat16 [16384, 2048], P('req'), may hold values from -10.5 to 10.5
- lengths: int32 [64], replicated, may hold values from 1 to 1024, 16384 in all
- dealing: int32 [64], replicated, may hold values from 0 to 63, each once
- norm_gain: bfloat16 [2048], replicated, may hold values from 0.5 to 1.5
- w_query: bfloat16 [2048, 2048], P(None, 'tp'), may hold values from -0.125 to 0.125
- w_key: bfloat16 [2048, 1024], P(None, 'tp'), may hold values from -0.125 to 0.125
- w_value: bfloat16 [2048, 1024], P(None, 'tp'), may hold values from -0.125 to 0.125
- query_gain: bfloat16 [128], replicated, may hold values from 0.5 to 8
- key_gain: bfloat16 [128], replicated, may hold values from 0.5 to 8
- w_out: bfloat16 [2048, 2048], P(None, 'tp'), may hold values from -0.125 to 0.125
Outputs:
- hidden_out: bfloat16 [16384, 2048], P('req', 'tp')
- kv_cache: bfloat16 [2, 64, 1024, 1024], P(None, 'req', None, 'tp')
Inputs may be any that keep to these rules, and one draw needn't show every extreme that they name: The lengths sum to 16384; the largest is exactly 1024. A permutation: dealt slot j, on device j of req, holds prompt dealing[j].
All inputs are finite; a program needn't handle non-finite values.
Results may differ from a plain program's by a relative error of at most 0.012.
The roundings to bfloat16 on the way count: a program that leaves them out, or rounds other values in their place, can miss the bound.
Values may be sent and summed in bfloat16 or wider, within the bound.
No kernel may reach another device: no remote copies, remote signals or barrier semaphores. Data moves between devices by JAX's collectives and lax.ppermute only.
A program may use at most 128 MiB of HBM per device.

v0:
```python
import jax
import jax.numpy as jnp
from jax import lax
from jax.sharding import PartitionSpec as P

EPS = 1e-06
THETA = 1000000.0


def rms_rows(values, scale_gain):
    inv_rms = lax.rsqrt(jnp.mean(values * values, axis=-1, keepdims=True) + EPS)
    return values * inv_rms * scale_gain


def rotate(values, positions):
    features = values.shape[-1]
    half_width = features // 2
    frequency = THETA ** (-(jnp.arange(half_width).astype(jnp.float32) * 2.0) / features)
    angles = positions.astype(jnp.float32)[:, None] * frequency[None, :]
    cosine = jnp.cos(angles)[:, None, :]
    sine_part = jnp.sin(angles)[:, None, :]
    first_half = values[..., :half_width]
    second_half = values[..., half_width:]
    return jnp.concatenate(
        [
            first_half * cosine - second_half * sine_part,
            second_half * cosine + first_half * sine_part,
        ],
        axis=-1,
    )


def project(normed, w_query, w_key, w_value, query_gain, key_gain, positions):
    head_dim = query_gain.shape[0]
    row_count = normed.shape[0]
    query_rows = jnp.dot(normed, w_query, preferred_element_type=jnp.float32).reshape(
        row_count, -1, head_dim
    )
    key_rows = jnp.dot(normed, w_key, preferred_element_type=jnp.float32).reshape(
        row_count, -1, head_dim
    )
    value_rows = jnp.dot(normed, w_value, preferred_element_type=jnp.float32).astype(jnp.bfloat16)
    query_rows = rotate(rms_rows(query_rows, query_gain.astype(jnp.float32)), positions).astype(
        jnp.bfloat16
    )
    key_rows = rotate(rms_rows(key_rows, key_gain.astype(jnp.float32)), positions).astype(
        jnp.bfloat16
    )
    return (query_rows.reshape(row_count, -1), key_rows.reshape(row_count, -1), value_rows)


def attend(query_slot, key_slot, value_slot, prompt_length, head_dim):
    slot_len, query_width = query_slot.shape
    kv_heads = key_slot.shape[1] // head_dim
    group_size = query_width // head_dim // kv_heads
    queries = query_slot.reshape(slot_len, kv_heads, group_size, head_dim)
    keys_split = key_slot.reshape(slot_len, kv_heads, head_dim)
    values_split = value_slot.reshape(slot_len, kv_heads, head_dim)
    scores = jnp.einsum(
        "qkgd,skd->kgqs", queries, keys_split, preferred_element_type=jnp.float32
    ) * head_dim ** (-0.5)
    offsets = jnp.arange(slot_len, dtype=jnp.int32)
    allowed = (offsets[None, :] <= offsets[:, None]) & (offsets[None, :] < prompt_length)
    scores = jnp.where(allowed[None, None], scores, -jnp.inf)
    row_max = jnp.max(scores, axis=-1, keepdims=True)
    weights = jnp.exp(scores - row_max)
    weights = (weights / jnp.sum(weights, axis=-1, keepdims=True)).astype(jnp.bfloat16)
    mixture = jnp.einsum(
        "kgqs,skd->qkgd", weights, values_split, preferred_element_type=jnp.float32
    )
    return mixture.astype(jnp.bfloat16).reshape(slot_len, query_width)


def on_device(
    hidden, lengths, dealing, norm_gain, w_query, w_key, w_value, query_gain, key_gain, w_out
):
    devices = lax.axis_size("req")
    home_index = lax.axis_index("req")
    slice_index = lax.axis_index("tp")
    tok_rows, features = hidden.shape
    head_dim = query_gain.shape[0]
    out_width = w_out.shape[1]
    q_width = w_query.shape[1]
    k_width = w_key.shape[1]
    slot_len = 4 * tok_rows
    capacity = slot_len // devices
    prompt_total = lengths.shape[0]
    prompt_ids = jnp.arange(prompt_total, dtype=jnp.int32)
    prompt_ends = jnp.cumsum(lengths)
    starts = prompt_ends - lengths
    packed_ids = jnp.arange(tok_rows, dtype=jnp.int32) * devices + home_index
    segment = jnp.sum((packed_ids[:, None] >= prompt_ends[None, :]).astype(jnp.int32), axis=1)
    seg_onehot = (segment[:, None] == prompt_ids[None, :]).astype(jnp.int32)
    positions = packed_ids - jnp.sum(seg_onehot * starts[None, :], axis=1)
    inverse = jnp.zeros((prompt_total,), jnp.int32).at[dealing].set(prompt_ids)
    deal_hot = (dealing[:, None] == prompt_ids[None, :]).astype(jnp.int32)
    dealt_starts = jnp.sum(deal_hot * starts[None, :], axis=1)
    dealt_lengths = jnp.sum(deal_hot * lengths[None, :], axis=1)
    first_offset = jnp.mod(home_index - dealt_starts, devices)
    ranks = jnp.arange(capacity, dtype=jnp.int32)
    slot_offset = first_offset[None, :] + ranks[:, None] * devices
    send_valid = slot_offset < dealt_lengths[None, :]
    send_rows = jnp.where(
        send_valid, (dealt_starts[None, :] + slot_offset - home_index) // devices, 0
    ).reshape(-1)
    my_start = lax.dynamic_index_in_dim(dealt_starts, home_index, 0, keepdims=False)
    my_length = lax.dynamic_index_in_dim(dealt_lengths, home_index, 0, keepdims=False)
    roll_shift = jnp.mod(my_start, devices)
    my_slots = jnp.sum(seg_onehot * inverse[None, :], axis=1)
    back_rows = positions // devices * devices + my_slots
    gain_values = norm_gain.astype(jnp.float32)
    normed = rms_rows(hidden.astype(jnp.float32), gain_values).astype(jnp.bfloat16)
    query_rows, key_rows, value_rows = project(
        normed, w_query, w_key, w_value, query_gain, key_gain, positions
    )
    qkv_rows = jnp.concatenate([query_rows, key_rows, value_rows], axis=1)
    picked = jnp.take(qkv_rows, send_rows, axis=0).reshape(capacity, devices, qkv_rows.shape[1])
    arrived = lax.all_to_all(
        jnp.where(send_valid[:, :, None], picked, jnp.zeros((), qkv_rows.dtype)),
        "req",
        split_axis=1,
        concat_axis=1,
        tiled=True,
    )
    slot_rows = jnp.roll(arrived, -roll_shift, axis=1).reshape(slot_len, arrived.shape[2])
    query_slot = slot_rows[:, :q_width]
    key_slot = slot_rows[:, q_width : q_width + k_width]
    value_slot = slot_rows[:, q_width + k_width :]
    mixture = attend(query_slot, key_slot, value_slot, my_length, head_dim)
    sendback = jnp.roll(mixture.reshape(capacity, devices, mixture.shape[1]), roll_shift, axis=1)
    returned = lax.all_to_all(sendback, "req", split_axis=1, concat_axis=1, tiled=True)
    attended = jnp.take(returned.reshape(capacity * devices, -1), back_rows, axis=0)
    kv_cache = jnp.stack([key_slot, value_slot])[:, None]
    summed = jnp.dot(
        lax.all_gather(attended, "tp", axis=1, tiled=True),
        w_out,
        preferred_element_type=jnp.float32,
    )
    branch = lax.optimization_barrier(summed.astype(jnp.bfloat16))
    residual = lax.dynamic_slice_in_dim(hidden, slice_index * out_width, out_width, 1)
    hidden_out = (residual.astype(jnp.float32) + branch.astype(jnp.float32)).astype(jnp.bfloat16)
    return (hidden_out, kv_cache)


def solution(mesh):
    in_specs = (
        P("req", None),
        P(),
        P(),
        P(),
        P(None, "tp"),
        P(None, "tp"),
        P(None, "tp"),
        P(),
        P(),
        P(None, "tp"),
    )
    out_specs = (P("req", "tp"), P(None, "req", None, "tp"))
    return jax.shard_map(
        on_device, mesh=mesh, in_specs=in_specs, out_specs=out_specs, check_vma=False
    )
```

profile of v0, /device:TPU:2, one launch (start us, length us, event | category | flops | bytes accessed | tf_op | source)
XLA Modules:
  0.0 212.4 jit_solution(9252795499204256088)
XLA Ops:
  7.2 0.9 copy.123
  8.3 0.7 sub.88
  9.0 0.8 select_reduce_fusion.2
  9.8 0.7 compare_select_fusion.7
  10.6 0.6 compare_and_fusion
  11.2 0.7 lt.124
  12.0 0.7 convert_element_type.73
  12.7 1.6 fusion.7
  14.3 2.2 %convolution_convert_fusion.1 = bf16[256,256]{0,1:T(8,128)(2,1)S(1)} fusion(bf16[2048,256]{1,0:T(8,128)(2,1)} %param.16, bf16[256,2048]{1,0:T(8,128)(2,1)} %param.10, f32[2048]{0:T(1024)S(1)} %convert_element_type.73, f32[256]{0:T(256)S(1)} %add_rsqrt_fusion.2), kind=kOutput, calls=%fused_computation.30 | convolution fusion | flops 270598144 | bytes 2237440 | tf_op jit(solution)/shard_map/dot_general | solution.py:42
  16.6 0.7 copy.131
  17.3 0.6 convert_element_type.79
  17.9 2.6 %multiply_reduce_fusion.1 = (f32[256,2]{0,1:T(2,128)S(1)}, f32[256,256]{0,1:T(8,128)}) fusion(bf16[2048,256]{1,0:T(8,128)(2,1)} %param.15, bf16[256,2048]{1,0:T(8,128)(2,1)S(1)} %copy-done.1, f32[2048]{0:T(1024)S(1)} %convert_element_type.73, f32[256]{0:T(256)S(1)} %add_rsqrt_fusion.2), kind=kOutput, calls=%fused_computation.42 | convolution fusion | flops 270663168 | bytes 2370560 | tf_op jit(solution)/shard_map/dot_general | solution.py:39
  20.5 0.6 add_rsqrt_fusion.1
  21.1 0.8 scatter_custom_fusion
  21.9 0.6 select_reduce_fusion
  23.7 1.1 multiply_multiply_fusion.1
  24.8 0.8 copy.149
  25.6 2.3 %fusion.29 = f32[256,512]{1,0:T(8,128)} fusion(bf16[2048,512]{1,0:T(8,128)(2,1)S(1)} %copy-done, bf16[256,2048]{1,0:T(8,128)(2,1)S(1)} %copy-done.1, f32[2048]{0:T(1024)} %copy-done.9, f32[256]{0:T(256)} %copy-done.14), kind=kOutput, calls=%fused_computation.107 | convolution fusion | flops 538968064 | bytes 3679232 | tf_op jit(solution)/shard_map/dot_general | solution.py:36
  27.8 1.2 reshape.456
  31.1 5.4 %gather_fusion = bf16[1024,1024]{1,0:T(8,128)(2,1)} fusion(bf16[256,1024]{1,0:T(8,128)(2,1)S(1)} %pad_maximum_fusion, s32[1024]{0:T(1024)S(1)} %broadcast_clamp_fusion), kind=kCustom, calls=%fused_computation | custom fusion | bytes 4198400 | tf_op jit(solution)/shard_map/jit(_take)/gather | solution.py:117
  36.5 4.0 %fusion.11 = bf16[16,64,1024]{2,0,1:T(8,128)(2,1)} fusion(bf16[16,64,1024]{2,1,0:T(8,128)(2,1)} %bitcast.61, pred[16,64]{0,1:T(8,128)(4,1)S(1)} %copy.125, pred[16,64]{0,1:T(8,128)(4,1)S(1)} %copy.124), kind=kLoop, calls=%fused_computation.25 | loop fusion | flops 2097152 | bytes 4196352 | tf_op jit(solution)/shard_map/jit(_where)/select_n | solution.py:119
  40.5 12.4 %all-to-all-start = ((bf16[16,64,1024]{2,0,1:T(8,128)(2,1)}), bf16[16,64,1024]{2,0,1:T(8,128)(2,1)}, u32[]{:S(2)}, u32[]{:S(2)}) async-start(bf16[16,64,1024]{2,0,1:T(8,128)(2,1)} %fusion.11), calls=%async_computation | async-start | bytes 4194304 | tf_op jit(solution)/shard_map/all_to_all | solution.py:118
  52.9 0.6 dynamic_slice.19
  55.5 0.6 dynamic_slice.21
  56.1 0.6 iota_compare_fusion.3
  56.7 1.3 fusion.6
  58.0 46.0 %all-to-all-done = bf16[16,64,1024]{2,0,1:T(8,128)(2,1)} async-done(((bf16[16,64,1024]{2,0,1:T(8,128)(2,1)}), bf16[16,64,1024]{2,0,1:T(8,128)(2,1)}, u32[]{:S(2)}, u32[]{:S(2)}) %all-to-all-start) | async-done | bytes 2097184 | tf_op jit(solution)/shard_map/all_to_all | solution.py:118
  104.0 2.7 %copy.133 = bf16[16,64,1024]{2,1,0:T(8,128)(2,1)S(1)} copy(bf16[16,64,1024]{2,0,1:T(8,128)(2,1)} %all-to-all-done) | data formatting | bytes 4194304 | tf_op jit(solution)/shard_map/all_to_all | solution.py:118
  106.8 1.6 fusion.10
  108.4 1.4 slice_bitcast_fusion
  109.9 2.0 copy.135
  112.0 2.1 copy.136
  114.0 1.3 copy.137
  115.3 11.2 %fusion.31 = (f32[2,2,1024]{2,1,0:T(2,128)S(1)}, f32[2,2,1024,1024]{2,3,1,0:T(8,128)}) fusion(pred[1024,1024]{0,1:T(8,128)(4,1)} %fusion.6, bf16[1024,2,128,1]{0,2,3,1:T(8,128)(2,1)} %bitcast.68, bf16[1024,2,2,128]{0,3,2,1:T(8,128)(2,1)} %bitcast.65), kind=kOutput, calls=%fused_computation.108 | convolution fusion | flops 1090520064 | bytes 19415040 | tf_op jit(solution)/shard_map/sub | solution.py:66
  126.5 7.2 %fusion.15 = bf16[1024,2,2,128]{0,3,2,1:T(8,128)(2,1)S(1)} fusion(bf16[1024,2,128,1]{0,2,3,1:T(8,128)(2,1)} %bitcast.67, f32[2,2,1024,1024]{2,3,1,0:T(8,128)} %get-tuple-element.35, f32[2,2,1024]{2,1,0:T(2,128)S(1)} %get-tuple-element.34), kind=kOutput, calls=%fused_computation.28 | convolution fusion | flops 1082654720 | bytes 18366464 | tf_op jit(solution)/shard_map/kgqs,skd->qkgd/dot_general | solution.py:68
  133.8 2.0 copy.141
  135.8 1.5 reshape_reshape.3
  137.3 0.8 fusion.16
  138.1 1.5 copy.142
  139.7 5.6 %all-to-all-start.1 = ((bf16[16,64,512]{2,0,1:T(8,128)(2,1)}), bf16[16,64,512]{2,0,1:T(8,128)(2,1)}, u32[]{:S(2)}, u32[]{:S(2)}) async-start(bf16[16,64,512]{2,0,1:T(8,128)(2,1)} %copy.142), calls=%async_computation.1 | async-start | bytes 2097152 | tf_op jit(solution)/shard_map/all_to_all | solution.py:131
  145.4 28.6 %all-to-all-done.1 = bf16[16,64,512]{2,0,1:T(8,128)(2,1)} async-done(((bf16[16,64,512]{2,0,1:T(8,128)(2,1)}), bf16[16,64,512]{2,0,1:T(8,128)(2,1)}, u32[]{:S(2)}, u32[]{:S(2)}) %all-to-all-start.1) | async-done | bytes 1048608 | tf_op jit(solution)/shard_map/all_to_all | solution.py:131
  174.0 1.8 copy.143
  175.8 1.2 gather_fusion.1
  176.9 0.8 broadcast_select_fusion
  177.8 2.3 %maximum_bitcast_fusion = bf16[2,1,1024,256]{3,2,1,0:T(8,128)(2,1)} fusion(bf16[1,1024,256]{2,1,0:T(8,128)(2,1)} %get-tuple-element.21, bf16[1,1024,256]{2,1,0:T(8,128)(2,1)} %get-tuple-element.20), kind=kLoop, calls=%fused_computation.32 | loop fusion | flops 524288 | bytes 2097152
  180.1 21.2 %all-gather.2.cloned.1.call-done = bf16[256,2048]{1,0:T(8,128)(2,1)} async-done(((bf16[256,512]{1,0:T(8,128)(2,1)}), bf16[256,2048]{1,0:T(8,128)(2,1)}) %all-gather.2.cloned.1.call-update) | async-done | bytes 1048592 | tf_op jit(solution)/shard_map/all_gather | solution.py:135
  201.2 2.6 %convolution_convert_fusion = bf16[256,512]{1,0:T(8,128)(2,1)S(1)} fusion(bf16[256,2048]{1,0:T(8,128)(2,1)} %all-gather.2.cloned.1.call-done, bf16[2048,512]{1,0:T(8,128)(2,1)} %param.19), kind=kOutput, calls=%fused_computation.29 | convolution fusion | flops 537001984 | bytes 3407872 | tf_op jit(solution)/shard_map/dot_general | solution.py:134
  203.8 1.7 add_convert_fusion
  (68 shorter events, 3.8 us)
Async XLA Ops:
  7.2 18.4 %copy-start = (bf16[2048,512]{1,0:T(8,128)(2,1)S(1)}, bf16[2048,512]{1,0:T(8,128)(2,1)}, u32[]{:S(2)}) copy-start(bf16[2048,512]{1,0:T(8,128)(2,1)} %param.14) | copy-start | bytes 6291460
  9.8 2.2 %copy-start.10 = (s32[64]{0:T(128)}, s32[64]{0:T(128)S(1)}, u32[]{:S(2)}) copy-start(s32[64]{0:T(128)S(1)} %get-tuple-element.19) | copy-start | bytes 772
  9.8 7.5 %copy-start.12 = (s32[64]{0:T(128)}, s32[64]{0:T(128)S(1)}, u32[]{:S(2)}) copy-start(s32[64]{0:T(128)S(1)} %get-tuple-element.18) | copy-start | bytes 772
  12.7 5.2 %copy-start.9 = (f32[2048]{0:T(1024)}, f32[2048]{0:T(1024)S(1)}, u32[]{:S(2)}) copy-start(f32[2048]{0:T(1024)S(1)} %convert_element_type.73) | copy-start | bytes 24580
  12.7 4.6 %copy-start.15 = (bf16[128]{0:T(256)(128)(2,1)S(1)}, bf16[128]{0:T(256)(128)(2,1)}, u32[]{:S(2)}) copy-start(bf16[128]{0:T(256)(128)(2,1)} %param.18) | copy-start | bytes 772
  12.7 5.2 %copy-start.1 = (bf16[256,2048]{1,0:T(8,128)(2,1)S(1)}, bf16[256,2048]{1,0:T(8,128)(2,1)}, u32[]{:S(2)}) copy-start(bf16[256,2048]{1,0:T(8,128)(2,1)} %param.10) | copy-start | bytes 3145732
  14.3 6.1 %copy-start.14 = (f32[256]{0:T(256)}, f32[256]{0:T(256)S(1)}, u32[]{:S(2)}) copy-start(f32[256]{0:T(256)S(1)} %add_rsqrt_fusion.2) | copy-start | bytes 3076
  22.6 0.6 copy-start.5
  25.6 3.5 %copy-start.16 = (bf16[128]{0:T(256)(128)(2,1)S(1)}, bf16[128]{0:T(256)(128)(2,1)}, u32[]{:S(2)}) copy-start(bf16[128]{0:T(256)(128)(2,1)} %param.17) | copy-start | bytes 772
  29.4 1.4 copy-start.4
  29.4 1.4 copy-start.8
  29.5 1.5 copy-start.2
  29.5 1.5 copy-start.3
  40.5 12.4 %copy-start.11 = (s32[64]{0:T(128)S(1)}, s32[64]{0:T(128)}, u32[]{:S(2)}) copy-start(s32[64]{0:T(128)} %copy-done.10) | copy-start | bytes 772
  40.5 15.0 %copy-start.13 = (s32[64]{0:T(128)S(1)}, s32[64]{0:T(128)}, u32[]{:S(2)}) copy-start(s32[64]{0:T(128)} %copy-done.12) | copy-start | bytes 772
  40.5 63.5 %all-to-all-start = ((bf16[16,64,1024]{2,0,1:T(8,128)(2,1)}), bf16[16,64,1024]{2,0,1:T(8,128)(2,1)}, u32[]{:S(2)}, u32[]{:S(2)}) async-start(bf16[16,64,1024]{2,0,1:T(8,128)(2,1)} %fusion.11), calls=%async_computation | async-start | bytes 4194304 | tf_op jit(solution)/shard_map/all_to_all | solution.py:118
  138.1 7.3 %copy-start.6 = (s32[256]{0:T(256)S(1)}, s32[256]{0:T(256)}, u32[]{:S(2)}) copy-start(s32[256]{0:T(256)} %copy-done.5) | copy-start | bytes 3076
  138.1 7.3 %copy-start.7 = (s32[256]{0:T(256)S(1)}, s32[256]{0:T(256)}, u32[]{:S(2)}) copy-start(s32[256]{0:T(256)} %get-tuple-element.16) | copy-start | bytes 3076
  139.7 34.3 %all-to-all-start.1 = ((bf16[16,64,512]{2,0,1:T(8,128)(2,1)}), bf16[16,64,512]{2,0,1:T(8,128)(2,1)}, u32[]{:S(2)}, u32[]{:S(2)}) async-start(bf16[16,64,512]{2,0,1:T(8,128)(2,1)} %copy.142), calls=%async_computation.1 | async-start | bytes 2097152 | tf_op jit(solution)/shard_map/all_to_all | solution.py:131
  145.3 55.9 %all-gather.2.cloned.1.call-start = ((), (), s32[]{:S(2)}) async-start(), calls=%async_computation.2 | async-start | bytes 1310720 | tf_op jit(solution)/shard_map/all_gather | solution.py:135
Sparse Core Ops, SparseCore 0:
  177.9 23.2 all-gather.1
where the time goes:
time: 213 us; the launch traced here: 212 us
  waiting for transfers between devices  95.7 us (45%)
  local copies, waits for them, and re-layouts  30.5 us (14%)
  matrix products  28.1 us (13%)
  other arithmetic  23.7 us (11%)
  starting transfers between devices  18 us (8%)
  between operations  16.4 us (8%)
    all_to_all x1, waiting for transfers between devices, on_device(): lax.all_to_all(jnp.where(send_valid[:, :, None], picked, jnp.zeros((), qk...  46 us
    all_to_all x1, waiting for transfers between devices, on_device(): lax.all_to_all(sendback, 'req', split_axis=1, concat_axis=1, tiled=True)  28.6 us
    all_gather x1, waiting for transfers between devices, on_device(): lax.all_gather(attended, 'tp', axis=1, tiled=True)  21.2 us
    all_to_all x1, starting transfers between devices, on_device(): lax.all_to_all(jnp.where(send_valid[:, :, None], picked, jnp.zeros((), qk...  12.4 us
    sub x1, matrix products, attend(): weights = jnp.exp(scores - row_max)  11.2 us
    dot_general x1, matrix products, attend(): jnp.einsum('kgqs,skd->qkgd', weights, values_split, preferred_element_typ...  7.24 us
    all_to_all x1, starting transfers between devices, on_device(): lax.all_to_all(sendback, 'req', split_axis=1, concat_axis=1, tiled=True)  5.63 us
    gather x1, local copies, waits for them, and re-layouts, on_device(): jnp.take(qkv_rows, send_rows, axis=0)  5.39 us
  transfers between devices with their start and end apart: 3, of which 3 were waited for; matrix products, arithmetic and copies ran while one was open for 3% of the time, Pallas kernels for 0%

commit v1 on v0

--- a/solution.py
+++ b/solution.py
@@ -132,7 +132,9 @@
     attended = jnp.take(returned.reshape(capacity * devices, -1), back_rows, axis=0)
     kv_cache = jnp.stack([key_slot, value_slot])[:, None]
     summed = jnp.dot(
-        lax.all_gather(attended, "tp", axis=1, tiled=True),
+        jnp.concatenate(
+            lax.all_to_all(jnp.stack([attended] * lax.axis_size("tp")), "tp", 0, 0), axis=1
+        ),
         w_out,
         preferred_element_type=jnp.float32,
     )

time: 213 us -> 198 us (0.930)
  between operations: 16.4 us -> 3.02 us
  waiting for transfers between devices: 95.7 us -> 87.8 us
  starting transfers between devices: 18 us -> 22.4 us
  local copies, waits for them, and re-layouts: 30.5 us -> 32.8 us
    all_gather x1 -> x0, waiting for transfers between devices: 21.2 us -> none  [on_device(): lax.all_gather(attended, 'tp', axis=1, tiled=True)]
    all_to_all x0 -> x1, waiting for transfers between devices: none -> 13.2 us  [on_device(): lax.all_to_all(jnp.stack([attended] * lax.axis_size('tp')), 'tp', 0, 0)]
    all_to_all x0 -> x1, starting transfers between devices: none -> 4.46 us  [on_device(): lax.all_to_all(jnp.stack([attended] * lax.axis_size('tp')), 'tp', 0, 0)]
  transfers between devices with their start and end apart: 3 -> 3, of which waited for: 3 -> 3; matrix products, arithmetic and copies ran while one was open for 3% -> 2% of each run, Pallas kernels for 0% -> 0%
where the time goes in v1:
time: 198 us; the launch traced here: 197 us
  waiting for transfers between devices  87.8 us (44%)
  local copies, waits for them, and re-layouts  32.8 us (17%)
  matrix products  28.1 us (14%)
  other arithmetic  22.5 us (11%)
  starting transfers between devices  22.4 us (11%)
  between operations  3.02 us (2%)
    all_to_all x1, waiting for transfers between devices, on_device(): lax.all_to_all(jnp.where(send_valid[:, :, None], picked, jnp.zeros((), qk...  46 us
    all_to_all x1, waiting for transfers between devices, on_device(): lax.all_to_all(sendback, 'req', split_axis=1, concat_axis=1, tiled=True)  28.6 us
    all_to_all x1, waiting for transfers between devices, on_device(): lax.all_to_all(jnp.stack([attended] * lax.axis_size('tp')), 'tp', 0, 0)  13.2 us
    all_to_all x1, starting transfers between devices, on_device(): lax.all_to_all(jnp.where(send_valid[:, :, None], picked, jnp.zeros((), qk...  12.4 us
    sub x1, matrix products, attend(): weights = jnp.exp(scores - row_max)  11.2 us
    dot_general x1, matrix products, attend(): jnp.einsum('kgqs,skd->qkgd', weights, values_split, preferred_element_typ...  7.24 us
    all_to_all x1, starting transfers between devices, on_device(): lax.all_to_all(sendback, 'req', split_axis=1, concat_axis=1, tiled=True)  5.63 us
    gather x1, local copies, waits for them, and re-layouts, on_device(): jnp.take(qkv_rows, send_rows, axis=0)  5.39 us
  transfers between devices with their start and end apart: 3, of which 3 were waited for; matrix products, arithmetic and copies ran while one was open for 2% of the time, Pallas kernels for 0%

profile of v1, /device:TPU:2, one launch (start us, length us, event | category | flops | bytes accessed | tf_op | source)
XLA Modules:
  0.0 196.6 jit_solution(6020284571209508463)
XLA Ops:
  0.7 0.9 copy.129
  1.8 0.7 sub.88
  2.4 0.8 select_reduce_fusion.2
  3.3 0.7 compare_select_fusion.7
  4.1 0.6 compare_and_fusion
  4.7 0.7 lt.124
  5.5 0.7 convert_element_type.73
  6.2 1.6 fusion.7
  7.8 2.2 %convolution_convert_fusion.1 = bf16[256,256]{0,1:T(8,128)(2,1)S(1)} fusion(bf16[2048,256]{1,0:T(8,128)(2,1)} %param.16, bf16[256,2048]{1,0:T(8,128)(2,1)} %param.10, f32[2048]{0:T(1024)S(1)} %convert_element_type.73, f32[256]{0:T(256)S(1)} %add_rsqrt_fusion.2), kind=kOutput, calls=%fused_computation.30 | convolution fusion | flops 270598144 | bytes 2237440 | tf_op jit(solution)/shard_map/dot_general | solution.py:42
  10.0 0.7 copy.137
  11.3 2.6 %multiply_reduce_fusion.1 = (f32[256,2]{0,1:T(2,128)S(1)}, f32[256,256]{0,1:T(8,128)}) fusion(bf16[2048,256]{1,0:T(8,128)(2,1)} %param.15, bf16[256,2048]{1,0:T(8,128)(2,1)S(1)} %copy-done.3, f32[2048]{0:T(1024)S(1)} %convert_element_type.73, f32[256]{0:T(256)S(1)} %add_rsqrt_fusion.2), kind=kOutput, calls=%fused_computation.42 | convolution fusion | flops 270663168 | bytes 2370560 | tf_op jit(solution)/shard_map/dot_general | solution.py:39
  14.6 0.8 scatter_custom_fusion
  15.4 0.6 select_reduce_fusion
  17.1 1.1 multiply_multiply_fusion.1
  18.3 0.8 copy.156
  19.0 2.3 %fusion.29 = f32[256,512]{1,0:T(8,128)} fusion(bf16[2048,512]{1,0:T(8,128)(2,1)S(1)} %copy-done, bf16[256,2048]{1,0:T(8,128)(2,1)S(1)} %copy-done.3, f32[2048]{0:T(1024)} %copy-done.11, f32[256]{0:T(256)} %copy-done.16), kind=kOutput, calls=%fused_computation.107 | convolution fusion | flops 538968064 | bytes 3679232 | tf_op jit(solution)/shard_map/dot_general | solution.py:36
  21.3 1.2 reshape.469
  24.5 5.4 %gather_fusion = bf16[1024,1024]{1,0:T(8,128)(2,1)} fusion(bf16[256,1024]{1,0:T(8,128)(2,1)S(1)} %pad_maximum_fusion, s32[1024]{0:T(1024)S(1)} %broadcast_clamp_fusion), kind=kCustom, calls=%fused_computation | custom fusion | bytes 4198400 | tf_op jit(solution)/shard_map/jit(_take)/gather | solution.py:117
  29.9 4.0 %fusion.11 = bf16[16,64,1024]{2,0,1:T(8,128)(2,1)} fusion(bf16[16,64,1024]{2,1,0:T(8,128)(2,1)} %bitcast.64, pred[16,64]{0,1:T(8,128)(4,1)S(1)} %copy.131, pred[16,64]{0,1:T(8,128)(4,1)S(1)} %copy.130), kind=kLoop, calls=%fused_computation.25 | loop fusion | flops 2097152 | bytes 4196352 | tf_op jit(solution)/shard_map/jit(_where)/select_n | solution.py:119
  34.0 12.4 %all-to-all-start = ((bf16[16,64,1024]{2,0,1:T(8,128)(2,1)}), bf16[16,64,1024]{2,0,1:T(8,128)(2,1)}, u32[]{:S(2)}, u32[]{:S(2)}) async-start(bf16[16,64,1024]{2,0,1:T(8,128)(2,1)} %fusion.11), calls=%async_computation | async-start | bytes 4194304 | tf_op jit(solution)/shard_map/all_to_all | solution.py:118
  46.4 0.6 dynamic_slice.19
  49.5 0.6 iota_compare_fusion.3
  50.2 1.3 fusion.6
  51.5 46.0 %all-to-all-done = bf16[16,64,1024]{2,0,1:T(8,128)(2,1)} async-done(((bf16[16,64,1024]{2,0,1:T(8,128)(2,1)}), bf16[16,64,1024]{2,0,1:T(8,128)(2,1)}, u32[]{:S(2)}, u32[]{:S(2)}) %all-to-all-start) | async-done | bytes 2097184 | tf_op jit(solution)/shard_map/all_to_all | solution.py:118
  97.5 2.7 %copy.139 = bf16[16,64,1024]{2,1,0:T(8,128)(2,1)S(1)} copy(bf16[16,64,1024]{2,0,1:T(8,128)(2,1)} %all-to-all-done) | data formatting | bytes 4194304 | tf_op jit(solution)/shard_map/all_to_all | solution.py:118
  100.2 1.6 fusion.10
  101.8 1.4 slice_bitcast_fusion
  103.4 2.0 %copy.141 = bf16[1024,256]{0,1:T(8,128)(2,1)} copy(bf16[1024,256]{1,0:T(8,128)(2,1)} %get-tuple-element.23) | data formatting | bytes 1048576 | tf_op jit(solution)/shard_map/slice | solution.py:128
  105.4 2.1 %copy.142 = bf16[1024,256]{0,1:T(8,128)(2,1)} copy(bf16[1024,256]{1,0:T(8,128)(2,1)} %get-tuple-element.22) | data formatting | bytes 1048576 | tf_op jit(solution)/shard_map/slice | solution.py:127
  107.5 1.3 copy.143
  108.8 11.2 %fusion.31 = (f32[2,2,1024]{2,1,0:T(2,128)S(1)}, f32[2,2,1024,1024]{2,3,1,0:T(8,128)}) fusion(pred[1024,1024]{0,1:T(8,128)(4,1)} %fusion.6, bf16[1024,2,128,1]{0,2,3,1:T(8,128)(2,1)} %bitcast.71, bf16[1024,2,2,128]{0,3,2,1:T(8,128)(2,1)} %bitcast.68), kind=kOutput, calls=%fused_computation.108 | convolution fusion | flops 1090520064 | bytes 19415040 | tf_op jit(solution)/shard_map/sub | solution.py:66
  120.0 7.2 %fusion.15 = bf16[1024,2,2,128]{0,3,2,1:T(8,128)(2,1)S(1)} fusion(bf16[1024,2,128,1]{0,2,3,1:T(8,128)(2,1)} %bitcast.70, f32[2,2,1024,1024]{2,3,1,0:T(8,128)} %get-tuple-element.35, f32[2,2,1024]{2,1,0:T(2,128)S(1)} %get-tuple-element.34), kind=kOutput, calls=%fused_computation.28 | convolution fusion | flops 1082654720 | bytes 18366464 | tf_op jit(solution)/shard_map/kgqs,skd->qkgd/dot_general | solution.py:68
  127.3 2.0 %copy.147 = bf16[1024,2,2,128]{3,2,1,0:T(2,128)(2,1)} copy(bf16[1024,2,2,128]{0,3,2,1:T(8,128)(2,1)S(1)} %fusion.15) | data formatting | bytes 2097152 | tf_op jit(solution)/shard_map/convert_element_type | solution.py:71
  129.3 1.5 reshape_reshape.3
  130.8 0.8 fusion.16
  131.6 1.5 copy.148
  133.1 5.6 %all-to-all-start.1 = ((bf16[16,64,512]{2,0,1:T(8,128)(2,1)}), bf16[16,64,512]{2,0,1:T(8,128)(2,1)}, u32[]{:S(2)}, u32[]{:S(2)}) async-start(bf16[16,64,512]{2,0,1:T(8,128)(2,1)} %copy.148), calls=%async_computation.1 | async-start | bytes 2097152 | tf_op jit(solution)/shard_map/all_to_all | solution.py:131
  138.9 28.6 %all-to-all-done.1 = bf16[16,64,512]{2,0,1:T(8,128)(2,1)} async-done(((bf16[16,64,512]{2,0,1:T(8,128)(2,1)}), bf16[16,64,512]{2,0,1:T(8,128)(2,1)}, u32[]{:S(2)}, u32[]{:S(2)}) %all-to-all-start.1) | async-done | bytes 1048608 | tf_op jit(solution)/shard_map/all_to_all | solution.py:131
  167.5 1.8 copy.149
  169.3 1.2 gather_fusion.1
  170.4 0.8 broadcast_select_fusion
  171.2 1.2 copy.150
  172.4 1.1 stack.16
  173.5 4.5 %all-to-all-start.2 = ((bf16[4,256,512]{1,2,0:T(8,128)(2,1)}), bf16[4,256,512]{1,2,0:T(8,128)(2,1)}, u32[]{:S(2)}, u32[]{:S(2)}) async-start(bf16[4,256,512]{1,2,0:T(8,128)(2,1)} %stack.16), calls=%async_computation.2 | async-start | bytes 2097152 | tf_op jit(solution)/shard_map/all_to_all | solution.py:136
  178.0 1.1 maximum_bitcast_fusion
  179.0 13.2 %all-to-all-done.2 = bf16[4,256,512]{1,2,0:T(8,128)(2,1)} async-done(((bf16[4,256,512]{1,2,0:T(8,128)(2,1)}), bf16[4,256,512]{1,2,0:T(8,128)(2,1)}, u32[]{:S(2)}, u32[]{:S(2)}) %all-to-all-start.2) | async-done | bytes 1048608 | tf_op jit(solution)/shard_map/all_to_all | solution.py:136
  192.2 2.6 %convolution_convert_fusion = bf16[256,512]{1,0:T(8,128)(2,1)S(1)} fusion(bf16[256,2048]{0,1:T(8,128)(2,1)} %bitcast.21, bf16[2048,512]{1,0:T(8,128)(2,1)} %param.19), kind=kOutput, calls=%fused_computation.29 | convolution fusion | flops 537001984 | bytes 3407872 | tf_op jit(solution)/shard_map/dot_general | solution.py:134
  194.9 1.7 add_convert_fusion
  (73 shorter events, 5.5 us)
Async XLA Ops:
  0.6 18.4 %copy-start = (bf16[2048,512]{1,0:T(8,128)(2,1)S(1)}, bf16[2048,512]{1,0:T(8,128)(2,1)}, u32[]{:S(2)}) copy-start(bf16[2048,512]{1,0:T(8,128)(2,1)} %param.14) | copy-start | bytes 6291460
  3.3 2.2 %copy-start.12 = (s32[64]{0:T(128)}, s32[64]{0:T(128)S(1)}, u32[]{:S(2)}) copy-start(s32[64]{0:T(128)S(1)} %get-tuple-element.19) | copy-start | bytes 772
  3.3 7.5 %copy-start.14 = (s32[64]{0:T(128)}, s32[64]{0:T(128)S(1)}, u32[]{:S(2)}) copy-start(s32[64]{0:T(128)S(1)} %get-tuple-element.18) | copy-start | bytes 772
  6.2 5.2 %copy-start.11 = (f32[2048]{0:T(1024)}, f32[2048]{0:T(1024)S(1)}, u32[]{:S(2)}) copy-start(f32[2048]{0:T(1024)S(1)} %convert_element_type.73) | copy-start | bytes 24580
  6.2 4.6 %copy-start.17 = (bf16[128]{0:T(256)(128)(2,1)S(1)}, bf16[128]{0:T(256)(128)(2,1)}, u32[]{:S(2)}) copy-start(bf16[128]{0:T(256)(128)(2,1)} %param.18) | copy-start | bytes 772
  6.2 5.2 %copy-start.3 = (bf16[256,2048]{1,0:T(8,128)(2,1)S(1)}, bf16[256,2048]{1,0:T(8,128)(2,1)}, u32[]{:S(2)}) copy-start(bf16[256,2048]{1,0:T(8,128)(2,1)} %param.10) | copy-start | bytes 3145732
  7.8 6.1 %copy-start.16 = (f32[256]{0:T(256)}, f32[256]{0:T(256)S(1)}, u32[]{:S(2)}) copy-start(f32[256]{0:T(256)S(1)} %add_rsqrt_fusion.2) | copy-start | bytes 3076
  16.0 0.6 copy-start.7
  19.0 3.5 %copy-start.18 = (bf16[128]{0:T(256)(128)(2,1)S(1)}, bf16[128]{0:T(256)(128)(2,1)}, u32[]{:S(2)}) copy-start(bf16[128]{0:T(256)(128)(2,1)} %param.17) | copy-start | bytes 772
  22.9 1.4 copy-start.6
  22.9 1.4 copy-start.10
  22.9 1.5 copy-start.4
  22.9 1.5 copy-start.5
  34.0 12.4 %copy-start.13 = (s32[64]{0:T(128)S(1)}, s32[64]{0:T(128)}, u32[]{:S(2)}) copy-start(s32[64]{0:T(128)} %copy-done.12) | copy-start | bytes 772
  34.0 15.0 %copy-start.15 = (s32[64]{0:T(128)S(1)}, s32[64]{0:T(128)}, u32[]{:S(2)}) copy-start(s32[64]{0:T(128)} %copy-done.14) | copy-start | bytes 772
  34.0 63.5 %all-to-all-start = ((bf16[16,64,1024]{2,0,1:T(8,128)(2,1)}), bf16[16,64,1024]{2,0,1:T(8,128)(2,1)}, u32[]{:S(2)}, u32[]{:S(2)}) async-start(bf16[16,64,1024]{2,0,1:T(8,128)(2,1)} %fusion.11), calls=%async_computation | async-start | bytes 4194304 | tf_op jit(solution)/shard_map/all_to_all | solution.py:118
  131.6 7.2 %copy-start.8 = (s32[256]{0:T(256)S(1)}, s32[256]{0:T(256)}, u32[]{:S(2)}) copy-start(s32[256]{0:T(256)} %copy-done.7) | copy-start | bytes 3076
  131.6 7.2 %copy-start.9 = (s32[256]{0:T(256)S(1)}, s32[256]{0:T(256)}, u32[]{:S(2)}) copy-start(s32[256]{0:T(256)} %get-tuple-element.16) | copy-start | bytes 3076
  133.1 34.3 %all-to-all-start.1 = ((bf16[16,64,512]{2,0,1:T(8,128)(2,1)}), bf16[16,64,512]{2,0,1:T(8,128)(2,1)}, u32[]{:S(2)}, u32[]{:S(2)}) async-start(bf16[16,64,512]{2,0,1:T(8,128)(2,1)} %copy.148), calls=%async_computation.1 | async-start | bytes 2097152 | tf_op jit(solution)/shard_map/all_to_all | solution.py:131
  171.2 6.7 %copy-start.1 = (bf16[1,1024,256]{2,1,0:T(8,128)(2,1)S(1)}, bf16[1,1024,256]{2,1,0:T(8,128)(2,1)}, u32[]{:S(2)}) copy-start(bf16[1,1024,256]{2,1,0:T(8,128)(2,1)} %get-tuple-element.20) | copy-start | bytes 1572868
  171.2 6.7 %copy-start.2 = (bf16[1,1024,256]{2,1,0:T(8,128)(2,1)S(1)}, bf16[1,1024,256]{2,1,0:T(8,128)(2,1)}, u32[]{:S(2)}) copy-start(bf16[1,1024,256]{2,1,0:T(8,128)(2,1)} %get-tuple-element.21) | copy-start | bytes 1572868
  173.5 18.7 %all-to-all-start.2 = ((bf16[4,256,512]{1,2,0:T(8,128)(2,1)}), bf16[4,256,512]{1,2,0:T(8,128)(2,1)}, u32[]{:S(2)}, u32[]{:S(2)}) async-start(bf16[4,256,512]{1,2,0:T(8,128)(2,1)} %stack.16), calls=%async_computation.2 | async-start | bytes 2097152 | tf_op jit(solution)/shard_map/all_to_all | solution.py:136
